TPU v7x, 32 devices: a whole 2x2x4 slice. The times are simulated.
32 devices in a mesh: section: 2 (over core), fsdp: 2 (over y), expert: 8 (over z, x).
Axes of the slice: x: 2, y: 2, z: 4, core: 2. Of those that a mesh axis runs over, the one named last changes fastest.
Arguments:
- tokens: bfloat16 [2048, 2048], P(('fsdp', 'expert')), may hold values from -40 to 40
- norm_gain: float32 [2, 2048], P('section'), may hold values from 0.5 to 1.5
- router: bfloat16 [2, 2048, 32], P('section'), may hold values from -0.3125 to 0.3125
- w_gate: bfloat16 [2, 32, 2048, 768], P('section', 'expert', 'fsdp'), may hold values from -0.125 to 0.125
- w_up: bfloat16 [2, 32, 2048, 768], P('section', 'expert', 'fsdp'), may hold values from -0.125 to 0.125
- w_down: bfloat16 [2, 32, 768, 2048], P('section', 'expert', None, 'fsdp'), may hold values from -0.21875 to 0.21875
- routes: int32 [2, 2048, 6], P('section', ('fsdp', 'expert')), may hold values from 0 to 31, all different within a row; in each aligned block of 64 rows (0 to 63, 64 to 127, ..., all dimensions but the last counted through in order) at most 14 rows name the same one
Outputs:
- final_out: bfloat16 [2048, 2048], P(('fsdp', 'expert'), 'section')
- layer_stats: float32 [2], P('section')
Inputs may be any that keep to these rules, and one draw needn't show every extreme that they name: `routes`: each row names 6 different experts; in every aligned block of 64 rows of one layer no expert is named by more than 14 rows, a bound that some block reaches.
All inputs are finite; a program needn't handle non-finite values.
Results may differ from a plain program's by a relative error of at most 0.0065.
Values may be sent and summed in bfloat16 or wider, within the bound.
No kernel may reach another device: no remote copies, remote signals or barrier semaphores. Data moves between devices by JAX's collectives and lax.ppermute only.
A program may use at most 192 MiB of HBM per device.

v0:
```python
import jax
import jax.numpy as jnp
from jax import lax
from jax.sharding import PartitionSpec as P

TOP = 6
BLOCK = 64
epsilon = 1e-06


def other_section(value):
    return lax.ppermute(value, "section", [(0, 1), (1, 0)])


def rms_scaled(hidden_rows, gain_row):
    values = hidden_rows.astype(jnp.float32)
    scale = lax.rsqrt(jnp.mean(values * values, axis=-1, keepdims=True) + epsilon)
    return (values * scale * gain_row).astype(jnp.bfloat16)


def gate_weights(normed, router_weight, route_rows):
    logits = jnp.dot(normed, router_weight, preferred_element_type=jnp.float32)
    scores = jax.nn.sigmoid(logits)
    expert_ids = jnp.arange(router_weight.shape[1], dtype=jnp.int32)
    chosen_mask = (route_rows[:, :, None] == expert_ids[None, None, :]).astype(jnp.float32)
    chosen = jnp.sum(scores[:, None, :] * chosen_mask, axis=2)
    return chosen / jnp.sum(chosen, axis=1, keepdims=True)


def slot_positions(route_rows, experts_count, capacity):
    flat_routes = route_rows.reshape(-1)
    onehot = (flat_routes[:, None] == jnp.arange(experts_count, dtype=jnp.int32)[None, :]).astype(
        jnp.int32
    )
    before = jnp.cumsum(onehot, axis=0) - onehot
    slot_index = jnp.sum(before * onehot, axis=1)
    return (flat_routes * capacity + slot_index).reshape(route_rows.shape)


def expert_layer(entering, route_rows, gain_row, router_weight, weights, capacity):
    gate_w, up_w, down_w = weights
    width = entering.shape[1]
    experts_count = router_weight.shape[1]
    local_experts, chunk, hidden_units = gate_w.shape
    fsdp_count = lax.axis_size("fsdp")
    expert_devices = lax.axis_size("expert")
    peers = fsdp_count * expert_devices
    normed = rms_scaled(entering, gain_row)
    mix_weights = gate_weights(normed, router_weight, route_rows)
    positions = slot_positions(route_rows, experts_count, capacity)
    slot_ids = jnp.arange(experts_count * capacity, dtype=jnp.int32)
    placing = jnp.any(positions[None, :, :] == slot_ids[:, None, None], axis=2).astype(jnp.bfloat16)
    buffer = jnp.dot(placing, normed, preferred_element_type=jnp.float32).astype(jnp.bfloat16)
    outgoing = (
        buffer.reshape(expert_devices, local_experts * capacity, fsdp_count, chunk)
        .transpose(2, 0, 1, 3)
        .reshape(peers, local_experts * capacity, chunk)
    )
    arrived = lax.all_to_all(outgoing, ("fsdp", "expert"), 0, 0, tiled=True)
    arrived = arrived.reshape(peers, local_experts, capacity, chunk)
    gate_part = jnp.einsum("sjcd,jdh->sjch", arrived, gate_w, preferred_element_type=jnp.float32)
    up_part = jnp.einsum("sjcd,jdh->sjch", arrived, up_w, preferred_element_type=jnp.float32)
    both = jnp.concatenate([gate_part, up_part], axis=-1)
    summed = lax.psum_scatter(both, "fsdp", scatter_dimension=0, tiled=True)
    gate_sum = summed[..., :hidden_units]
    up_sum = summed[..., hidden_units:]
    inner_act = (jax.nn.silu(gate_sum) * up_sum).astype(jnp.bfloat16)
    inner_all = lax.all_gather(inner_act, "fsdp", axis=0, tiled=True)
    produced = jnp.einsum(
        "sjch,jhd->sjcd", inner_all, down_w, preferred_element_type=jnp.float32
    ).astype(jnp.bfloat16)
    returned = lax.all_to_all(
        produced.reshape(peers, local_experts * capacity, chunk),
        ("fsdp", "expert"),
        0,
        0,
        tiled=True,
    )
    flat_out = (
        returned.reshape(fsdp_count, expert_devices, local_experts * capacity, chunk)
        .transpose(1, 2, 0, 3)
        .reshape(experts_count * capacity, width)
    )
    picked = jnp.take(flat_out, positions, axis=0)
    branch_sum = jnp.sum(mix_weights[:, :, None] * picked.astype(jnp.float32), axis=1)
    return (entering.astype(jnp.float32) + branch_sum).astype(jnp.bfloat16)


def body(tokens, norm_gain, router, w_gate, w_up, w_down, routes):
    section_index = lax.axis_index("section")
    sections = lax.axis_size("section")
    token_rows, width = tokens.shape
    piece = token_rows // sections
    experts_count = router.shape[2]
    block_capacity = (7 * BLOCK * TOP + 6 * experts_count - 1) // (6 * experts_count)
    capacity = block_capacity * (piece // BLOCK)
    own_weights = (w_gate[0], w_up[0], w_down[0])
    other_weights = tuple((other_section(w) for w in own_weights))
    own_small = (norm_gain[0], router[0], routes[0])
    other_small = tuple((other_section(v) for v in own_small))
    hidden = lax.dynamic_slice_in_dim(tokens, section_index * piece, piece, 0)
    squares = []
    for layer in range(sections):
        mine = section_index == layer
        gain_row, router_weight, route_all = [
            jnp.where(mine, a, b) for a, b in zip(own_small, other_small)
        ]
        weights = tuple((jnp.where(mine, a, b) for a, b in zip(own_weights, other_weights)))
        route_rows = lax.dynamic_slice_in_dim(route_all, section_index * piece, piece, 0)
        hidden = expert_layer(hidden, route_rows, gain_row, router_weight, weights, capacity)
        values = hidden.astype(jnp.float32)
        squares.append(jnp.sum(values * values))
    totals = lax.psum(jnp.stack(squares), ("section", "fsdp", "expert"))
    token_total = token_rows * lax.axis_size("fsdp") * lax.axis_size("expert")
    stats = jnp.sqrt(totals / (token_total * width))
    layer_stats = lax.dynamic_slice_in_dim(stats, section_index, 1, 0)
    half_width = width // 2
    keep = lax.dynamic_slice_in_dim(hidden, section_index * half_width, half_width, 1)
    send = lax.dynamic_slice_in_dim(hidden, (1 - section_index) * half_width, half_width, 1)
    arrived = other_section(send)
    final_out = jnp.where(
        section_index == 0,
        jnp.concatenate([keep, arrived], axis=0),
        jnp.concatenate([arrived, keep], axis=0),
    )
    return (final_out, layer_stats)


def solution(mesh):
    in_specs = (
        P(("fsdp", "expert"), None),
        P("section", None),
        P("section", None, None),
        P("section", "expert", "fsdp", None),
        P("section", "expert", "fsdp", None),
        P("section", "expert", None, "fsdp"),
        P("section", ("fsdp", "expert"), None),
    )
    out_specs = (P(("fsdp", "expert"), "section"), P("section"))
    return jax.shard_map(body, mesh=mesh, in_specs=in_specs, out_specs=out_specs, check_vma=False)
```

profile of v0, /device:TPU:0, one launch (start us, length us, event | category | flops | bytes accessed | tf_op | source)
XLA Modules:
  0.0 542.5 jit_solution(15079160899732492798)
XLA Ops:
  10.1 7.8 %collective-permute-done = s32[128,6]{0,1:T(8,128)S(1)} collective-permute-done((s32[128,6]{0,1:T(8,128)S(1)}, s32[128,6]{0,1:T(8,128)S(1)}, u32[]{:S(2)}, u32[]{:S(2)}) %collective-permute-start) | collective-permute-done | bytes 3104 | tf_op jit(solution)/shard_map/ppermute | solution.py:12
  24.3 4.6 reshape.156
  29.5 52.1 %all_to_all.20 = bf16[16,56,1024]{2,1,0:T(8,128)(2,1)S(1)} all-to-all(bf16[16,56,1024]{2,1,0:T(8,128)(2,1)S(1)} %bitcast.172), channel_id=1, replica_groups=mesh['section'=2,'fsdp'=2,'expert'=8] {'fsdp','expert'}, dimensions={0} | all-to-all | bytes 3670016 | tf_op jit(solution)/shard_map/all_to_all | solution.py:59
  82.6 4.6 fusion.27
  87.1 4.6 fusion.30
  91.7 3.1 pad_maximum_fusion
  97.3 66.4 %reduce-scatter.3.cloned.1.call-done = f32[8,4,14,1536]{3,0,2,1:T(8,128)} async-done(((f32[16,4,14,1536]{3,0,2,1:T(8,128)}), f32[8,4,14,1536]{3,0,2,1:T(8,128)}) %reduce-scatter.3.cloned.1.call-update) | async-done | bytes 2752528 | tf_op jit(solution)/shard_map/reduce_scatter | solution.py:64
  163.7 3.0 fusion.43
  166.8 25.1 %all-gather.3.cloned.1.call-done = bf16[16,4,14,768]{3,0,2,1:T(8,128)(2,1)} async-done(((bf16[8,4,14,768]{3,0,2,1:T(8,128)(2,1)}), bf16[16,4,14,768]{3,0,2,1:T(8,128)(2,1)}) %all-gather.3.cloned.1.call-update) | async-done | bytes 1376272 | tf_op jit(solution)/shard_map/all_gather | solution.py:68
  191.9 4.9 fusion.24
  199.1 5.7 %all-to-all-start.1 = ((bf16[16,56,1024]{2,1,0:T(8,128)(2,1)}), bf16[16,56,1024]{2,1,0:T(8,128)(2,1)S(1)}, u32[]{:S(2)}, u32[]{:S(2)}) async-start(bf16[16,56,1024]{2,1,0:T(8,128)(2,1)} %copy.68), calls=%async_computation.2 | async-start | bytes 3670016 | tf_op jit(solution)/shard_map/all_to_all | solution.py:72
  209.0 39.2 %all-to-all-done.1 = bf16[16,56,1024]{2,1,0:T(8,128)(2,1)S(1)} async-done(((bf16[16,56,1024]{2,1,0:T(8,128)(2,1)}), bf16[16,56,1024]{2,1,0:T(8,128)(2,1)S(1)}, u32[]{:S(2)}, u32[]{:S(2)}) %all-to-all-start.1) | async-done | bytes 1835040 | tf_op jit(solution)/shard_map/all_to_all | solution.py:72
  254.7 4.2 multiply_reduce_fusion.1
  264.7 49.3 %all_to_all.21 = bf16[16,56,1024]{2,1,0:T(8,128)(2,1)S(1)} all-to-all(bf16[16,56,1024]{2,1,0:T(8,128)(2,1)S(1)} %bitcast.174), channel_id=1, replica_groups=mesh['section'=2,'fsdp'=2,'expert'=8] {'fsdp','expert'}, dimensions={0} | all-to-all | bytes 3670016 | tf_op jit(solution)/shard_map/all_to_all | solution.py:59
  315.0 6.4 %fusion.36 = f32[16,4,14,768]{3,0,2,1:T(8,128)S(1)} fusion(bf16[16,4,14,1024]{3,0,2,1:T(8,128)(2,1)S(1)} %bitcast.178, bf16[4,1024,768]{2,1,0:T(8,128)(2,1)} %collective-permute-done.4, pred[]{:T(512)S(6)} %eq.124, bf16[1,4,1024,768]{3,2,1,0:T(8,128)(2,1)} %param.12), kind=kOutput, calls=%fused_computation.36 | convolution fusion | flops 1412431872 | bytes 17170432 | tf_op jit(solution)/shard_map/sjcd,jdh->sjch/dot_general | solution.py:61
  321.4 6.4 %fusion.39 = f32[16,4,14,768]{3,0,2,1:T(8,128)S(1)} fusion(bf16[16,4,14,1024]{3,0,2,1:T(8,128)(2,1)S(1)} %bitcast.179, bf16[4,1024,768]{2,1,0:T(8,128)(2,1)} %collective-permute-done.5, pred[]{:T(512)S(6)} %eq.124, bf16[1,4,1024,768]{3,2,1,0:T(8,128)(2,1)} %param.13), kind=kOutput, calls=%fused_computation.37 | convolution fusion | flops 1412431872 | bytes 17170432 | tf_op jit(solution)/shard_map/sjcd,jdh->sjch/dot_general | solution.py:62
  327.8 3.1 pad_maximum_fusion.1
  331.0 66.3 %reduce-scatter.5.cloned.1.call-done = f32[8,4,14,1536]{3,0,2,1:T(8,128)} async-done(((f32[16,4,14,1536]{3,0,2,1:T(8,128)}), f32[8,4,14,1536]{3,0,2,1:T(8,128)}) %reduce-scatter.5.cloned.1.call-update) | async-done | bytes 2752528 | tf_op jit(solution)/shard_map/reduce_scatter | solution.py:64
  400.3 25.1 %all-gather.5.cloned.1.call-done = bf16[16,4,14,768]{3,0,2,1:T(8,128)(2,1)} async-done(((bf16[8,4,14,768]{3,0,2,1:T(8,128)(2,1)}), bf16[16,4,14,768]{3,0,2,1:T(8,128)(2,1)}) %all-gather.5.cloned.1.call-update) | async-done | bytes 1376272 | tf_op jit(solution)/shard_map/all_gather | solution.py:68
  425.5 6.7 %fusion.33 = bf16[4,1024,16,14]{1,2,3,0:T(8,128)(2,1)S(1)} fusion(bf16[16,4,14,768]{3,0,2,1:T(8,128)(2,1)} %all-gather.5.cloned.1.call-done, bf16[4,768,1024]{2,1,0:T(8,128)(2,1)} %collective-permute-done.3, pred[]{:T(512)S(6)} %eq.124, bf16[1,4,768,1024]{3,2,1,0:T(8,128)(2,1)} %param.14), kind=kOutput, calls=%fused_computation.35 | convolution fusion | flops 1413349376 | bytes 15794177 | tf_op jit(solution)/shard_map/sjch,jhd->sjcd/dot_general | solution.py:69
  434.4 6.0 %all-to-all-start.3 = ((bf16[16,56,1024]{2,1,0:T(8,128)(2,1)}), bf16[16,56,1024]{2,1,0:T(8,128)(2,1)S(1)}, u32[]{:S(2)}, u32[]{:S(2)}) async-start(bf16[16,56,1024]{2,1,0:T(8,128)(2,1)} %copy.79), calls=%async_computation.5 | async-start | bytes 3670016 | tf_op jit(solution)/shard_map/all_to_all | solution.py:72
  441.3 40.0 %all-to-all-done.3 = bf16[16,56,1024]{2,1,0:T(8,128)(2,1)S(1)} async-done(((bf16[16,56,1024]{2,1,0:T(8,128)(2,1)}), bf16[16,56,1024]{2,1,0:T(8,128)(2,1)S(1)}, u32[]{:S(2)}, u32[]{:S(2)}) %all-to-all-start.3) | async-done | bytes 1835040 | tf_op jit(solution)/shard_map/all_to_all | solution.py:72
  487.8 4.2 multiply_reduce_fusion
  494.1 39.4 %psum.7 = f32[2]{0:T(128)S(1)} all-reduce(f32[2]{0:T(128)S(1)} %pad_maximum_fusion.2), channel_id=1, replica_groups=mesh['section'=2,'fsdp'=2,'expert'=8] {'section','fsdp','expert'}, use_global_device_ids=true, to_apply=%region_20.22 | all-reduce | flops 2 | bytes 16 | tf_op jit(solution)/shard_map/psum | solution.py:113
  (111 shorter events, 49.9 us)
Async XLA Ops:
  7.2 156.6 %reduce-scatter.3.cloned.1.call-start = ((), (), s32[]{:S(2)}) async-start(), calls=%async_computation.6 | async-start | bytes 8257536 | tf_op jit(solution)/shard_map/reduce_scatter | solution.py:64
  7.2 75.3 %collective-permute-start.4 = (bf16[4,1024,768]{2,1,0:T(8,128)(2,1)}, bf16[4,1024,768]{2,1,0:T(8,128)(2,1)}, u32[]{:S(2)}, u32[]{:S(2)}) collective-permute-start(bf16[4,1024,768]{2,1,0:T(8,128)(2,1)} %bitcast.187), channel_id=1, source_target_pairs={{0,16},{16,0},{1,17},{17,1},{2,18},{18,2},{3,19},{19,3},{4,20},{20... | collective-permute-start | bytes 18874376 | tf_op jit(solution)/shard_map/ppermute | solution.py:12
  8.5 9.4 %collective-permute-start = (s32[128,6]{0,1:T(8,128)S(1)}, s32[128,6]{0,1:T(8,128)S(1)}, u32[]{:S(2)}, u32[]{:S(2)}) collective-permute-start(s32[128,6]{0,1:T(8,128)S(1)} %bitcast.186), channel_id=1, source_target_pairs={{0,16},{16,0},{1,17},{17,1},{2,18},{18,2},{3,19},{19,3},{4,20},{20... | collective-permute-start | bytes 9224 | tf_op jit(solution)/shard_map/ppermute | solution.py:12
  8.5 12.2 %collective-permute-start.1 = (f32[2048]{0:T(1024)}, f32[2048]{0:T(1024)S(1)}, u32[]{:S(2)}, u32[]{:S(2)}) collective-permute-start(f32[2048]{0:T(1024)} %bitcast.184), channel_id=1, source_target_pairs={{0,16},{16,0},{1,17},{17,1},{2,18},{18,2},{3,19},{19,3},{4,20},{20... | collective-permute-start | bytes 24584 | tf_op jit(solution)/shard_map/ppermute | solution.py:12
  9.0 78.2 %collective-permute-start.5 = (bf16[4,1024,768]{2,1,0:T(8,128)(2,1)}, bf16[4,1024,768]{2,1,0:T(8,128)(2,1)}, u32[]{:S(2)}, u32[]{:S(2)}) collective-permute-start(bf16[4,1024,768]{2,1,0:T(8,128)(2,1)} %bitcast.188), channel_id=1, source_target_pairs={{0,16},{16,0},{1,17},{17,1},{2,18},{18,2},{3,19},{19,3},{4,20},{20... | collective-permute-start | bytes 18874376 | tf_op jit(solution)/shard_map/ppermute | solution.py:12
  94.8 97.1 %all-gather.3.cloned.1.call-start = ((), (), s32[]{:S(2)}) async-start(), calls=%async_computation.7 | async-start | bytes 2064384 | tf_op jit(solution)/shard_map/all_gather | solution.py:68
  95.3 71.4 %collective-permute-start.3 = (bf16[4,768,1024]{2,1,0:T(8,128)(2,1)}, bf16[4,768,1024]{2,1,0:T(8,128)(2,1)}, u32[]{:S(2)}, u32[]{:S(2)}) collective-permute-start(bf16[4,768,1024]{2,1,0:T(8,128)(2,1)} %bitcast.189), channel_id=1, source_target_pairs={{0,16},{16,0},{1,17},{17,1},{2,18},{18,2},{3,19},{19,3},{4,20},{20... | collective-permute-start | bytes 18874376 | tf_op jit(solution)/shard_map/ppermute | solution.py:12
  199.1 5.8 %copy-start.4 = (bf16[1,2048,32]{1,2,0:T(8,128)(2,1)S(1)}, bf16[1,2048,32]{1,2,0:T(8,128)(2,1)}, u32[]{:S(2)}) copy-start(bf16[1,2048,32]{1,2,0:T(8,128)(2,1)} %param.11) | copy-start | bytes 393220
  199.1 9.5 %copy-start.2 = (bf16[128,2048]{1,0:T(8,128)(2,1)S(1)}, bf16[128,2048]{1,0:T(8,128)(2,1)}, u32[]{:S(2)}) copy-start(bf16[128,2048]{1,0:T(8,128)(2,1)} %param.9) | copy-start | bytes 1572868
  199.1 49.1 %all-to-all-start.1 = ((bf16[16,56,1024]{2,1,0:T(8,128)(2,1)}), bf16[16,56,1024]{2,1,0:T(8,128)(2,1)S(1)}, u32[]{:S(2)}, u32[]{:S(2)}) async-start(bf16[16,56,1024]{2,1,0:T(8,128)(2,1)} %copy.68), calls=%async_computation.2 | async-start | bytes 3670016 | tf_op jit(solution)/shard_map/all_to_all | solution.py:72
  204.8 192.5 %reduce-scatter.5.cloned.1.call-start = ((), (), s32[]{:S(2)}) async-start(), calls=%async_computation.8 | async-start | bytes 8257536 | tf_op jit(solution)/shard_map/reduce_scatter | solution.py:64
  204.9 3.7 collective-permute-start.2
  208.6 42.0 %copy-start.6 = (bf16[2048,32]{0,1:T(8,128)(2,1)}, bf16[2048,32]{0,1:T(8,128)(2,1)S(1)}, u32[]{:S(2)}) copy-start(bf16[2048,32]{0,1:T(8,128)(2,1)S(1)} %collective-permute-done.2) | copy-start | bytes 393220
  253.1 5.8 %copy-start.3 = (bf16[128,2048]{1,0:T(8,128)(2,1)S(1)}, bf16[128,2048]{1,0:T(8,128)(2,1)}, u32[]{:S(2)}) copy-start(bf16[128,2048]{1,0:T(8,128)(2,1)} %param.9) | copy-start | bytes 1572868
  259.7 181.1 %copy-start = (bf16[64,2048]{1,0:T(8,128)(2,1)}, bf16[64,2048]{1,0:T(8,128)(2,1)S(1)}, u32[]{:S(2)}) copy-start(bf16[64,2048]{1,0:T(8,128)(2,1)S(1)} %get-tuple-element.13) | copy-start | bytes 786436
  331.0 94.5 %all-gather.5.cloned.1.call-start = ((), (), s32[]{:S(2)}) async-start(), calls=%async_computation.9 | async-start | bytes 2064384 | tf_op jit(solution)/shard_map/all_gather | solution.py:68
  434.4 6.4 %copy-start.5 = (bf16[1,2048,32]{1,2,0:T(8,128)(2,1)S(1)}, bf16[1,2048,32]{1,2,0:T(8,128)(2,1)}, u32[]{:S(2)}) copy-start(bf16[1,2048,32]{1,2,0:T(8,128)(2,1)} %param.11) | copy-start | bytes 393220
  434.4 6.4 %copy-start.7 = (bf16[2048,32]{0,1:T(8,128)(2,1)S(1)}, bf16[2048,32]{0,1:T(8,128)(2,1)}, u32[]{:S(2)}) copy-start(bf16[2048,32]{0,1:T(8,128)(2,1)} %copy-done.6) | copy-start | bytes 393220
  434.4 46.8 %all-to-all-start.3 = ((bf16[16,56,1024]{2,1,0:T(8,128)(2,1)}), bf16[16,56,1024]{2,1,0:T(8,128)(2,1)S(1)}, u32[]{:S(2)}, u32[]{:S(2)}) async-start(bf16[16,56,1024]{2,1,0:T(8,128)(2,1)} %copy.79), calls=%async_computation.5 | async-start | bytes 3670016 | tf_op jit(solution)/shard_map/all_to_all | solution.py:72
  486.1 5.9 %copy-start.1 = (bf16[64,2048]{1,0:T(8,128)(2,1)S(1)}, bf16[64,2048]{1,0:T(8,128)(2,1)}, u32[]{:S(2)}) copy-start(bf16[64,2048]{1,0:T(8,128)(2,1)} %copy-done) | copy-start | bytes 786436
  533.6 1.4 collective-permute-start.6
Sparse Core Ops, SparseCore 0:
  94.9 68.7 reduce-scatter.2
  166.9 24.9 all-gather.2
  331.1 66.1 reduce-scatter.4
  400.5 24.9 all-gather.4
where the time goes:
time: 550 us; the launch traced here: 543 us
  waiting for transfers between devices  271 us (49%)
  blocking collectives  141 us (26%)
  matrix products  37.7 us (7%)
  local copies, waits for them, and re-layouts  32.7 us (6%)
  other arithmetic  29.4 us (5%)
  starting transfers between devices  16.7 us (3%)
  between operations  14.4 us (3%)
    reduce_scatter x2, waiting for transfers between devices, expert_layer(): summed = lax.psum_scatter(both, 'fsdp', scatter_dimension=0, tiled=True)  133 us
    all_to_all x2, blocking collectives, expert_layer(): arrived = lax.all_to_all(outgoing, ('fsdp', 'expert'), 0, 0, tiled=True)  101 us
    all_to_all x2, waiting for transfers between devices, expert_layer(): lax.all_to_all(produced.reshape(peers, local_experts * capacity, chunk),...  79.2 us
    all_gather x2, waiting for transfers between devices, expert_layer(): inner_all = lax.all_gather(inner_act, 'fsdp', axis=0, tiled=True)  50.3 us
    psum x1, blocking collectives, body(): totals = lax.psum(jnp.stack(squares), ('section', 'fsdp', 'expert'))  39.4 us
    all_to_all x2, starting transfers between devices, expert_layer(): lax.all_to_all(produced.reshape(peers, local_experts * capacity, chunk),...  11.7 us
    dot_general x2, matrix products, expert_layer(): jnp.einsum('sjch,jhd->sjcd', inner_all, down_w, preferred_element_type=jn...  11.6 us
  transfers between devices with their start and end apart: 13, of which 8 were waited for; matrix products, arithmetic and copies ran while one was open for 5% of the time, Pallas kernels for 0%

commit v1 on v0

--- a/solution.py
+++ b/solution.py
@@ -6,6 +6,25 @@
 TOP = 6
 BLOCK = 64
 epsilon = 1e-06
+
+
+def _load_cycles(w_in, dim_at):
+    u_next = list(w_in.shape[1:])
+    u_next[dim_at] *= w_in.shape[0]
+    return jnp.moveaxis(w_in, 0, dim_at).reshape(u_next)
+
+
+def _make_things(u_in, bus_axis):
+    workers = lax.axis_size(bus_axis)
+    earlier = u_in[None]
+    for nth in range(workers.bit_length() - 1):
+        upper = 1 << nth
+        z = lax.ppermute(earlier, bus_axis, [(src_i, src_i ^ upper) for src_i in range(workers)])
+        vec_out = jnp.stack([earlier, z])
+        local_part = lax.axis_index(bus_axis)
+        x_now = local_part >> nth & 1
+        earlier = jnp.where(x_now == 0, vec_out, vec_out[::-1]).reshape(-1, *u_in.shape)
+    return earlier
 
 
 def other_section(value):
@@ -65,7 +84,11 @@
     gate_sum = summed[..., :hidden_units]
     up_sum = summed[..., hidden_units:]
     inner_act = (jax.nn.silu(gate_sum) * up_sum).astype(jnp.bfloat16)
-    inner_all = lax.all_gather(inner_act, "fsdp", axis=0, tiled=True)
+
+    def resolve_pipes(base_x, sheet, axis_no=0):
+        return _load_cycles(_make_things(base_x, sheet), axis_no)
+
+    inner_all = resolve_pipes(inner_act, "fsdp")
     produced = jnp.einsum(
         "sjch,jhd->sjcd", inner_all, down_w, preferred_element_type=jnp.float32
     ).astype(jnp.bfloat16)

time: 550 us -> 529 us (0.962)
  waiting for transfers between devices: 271 us -> 253 us
    all_gather x2 -> x0, waiting for transfers between devices: 50.3 us -> none  [expert_layer(): inner_all = lax.all_gather(inner_act, 'fsdp', axis=0, tiled=True)]
    ppermute x0 -> x2, waiting for transfers between devices: none -> 32.7 us  [_make_things(): lax.ppermute(earlier, bus_axis, [(src_i, src_i ^ upper) for src_i in rang...]
    convert_element_type x2 -> x0, other arithmetic: 6.03 us -> none  [expert_layer(): inner_act = (jax.nn.silu(gate_sum) * up_sum).astype(jnp.bfloat16)]
where the time goes in v1:
time: 529 us; the launch traced here: 525 us
  waiting for transfers between devices  253 us (48%)
  blocking collectives  140 us (26%)
  matrix products  37 us (7%)
  local copies, waits for them, and re-layouts  32.7 us (6%)
  other arithmetic  30.5 us (6%)
  starting transfers between devices  16.7 us (3%)
  between operations  14.7 us (3%)
    reduce_scatter x2, waiting for transfers between devices, expert_layer(): summed = lax.psum_scatter(both, 'fsdp', scatter_dimension=0, tiled=True)  133 us
    all_to_all x2, blocking collectives, expert_layer(): arrived = lax.all_to_all(outgoing, ('fsdp', 'expert'), 0, 0, tiled=True)  101 us
    all_to_all x2, waiting for transfers between devices, expert_layer(): lax.all_to_all(produced.reshape(peers, local_experts * capacity, chunk),...  78.1 us
    psum x1, blocking collectives, body(): totals = lax.psum(jnp.stack(squares), ('section', 'fsdp', 'expert'))  39.4 us
    ppermute x2, waiting for transfers between devices, _make_things(): lax.ppermute(earlier, bus_axis, [(src_i, src_i ^ upper) for src_i in rang...  32.7 us
    all_to_all x2, starting transfers between devices, expert_layer(): lax.all_to_all(produced.reshape(peers, local_experts * capacity, chunk),...  11.7 us
    dot_general x2, matrix products, expert_layer(): jnp.einsum('sjch,jhd->sjcd', inner_all, down_w, preferred_element_type=jn...  10.9 us
    dot_general x2, matrix products, expert_layer(): jnp.einsum('sjcd,jdh->sjch', arrived, up_w, preferred_element_type=jnp.fl...  10.9 us
  transfers between devices with their start and end apart: 13, of which 8 were waited for; matrix products, arithmetic and copies ran while one was open for 5% of the time, Pallas kernels for 0%

profile of v1, /device:TPU:0, one launch (start us, length us, event | category | flops | bytes accessed | tf_op | source)
XLA Modules:
  0.0 524.6 jit_solution(14855121201504157841)
XLA Ops:
  10.1 7.8 %collective-permute-done = s32[128,6]{0,1:T(8,128)S(1)} collective-permute-done((s32[128,6]{0,1:T(8,128)S(1)}, s32[128,6]{0,1:T(8,128)S(1)}, u32[]{:S(2)}, u32[]{:S(2)}) %collective-permute-start) | collective-permute-done | bytes 3104 | tf_op jit(solution)/shard_map/ppermute | solution.py:31
  24.3 4.6 reshape.156
  29.5 52.4 %all_to_all.20 = bf16[16,56,1024]{2,1,0:T(8,128)(2,1)S(1)} all-to-all(bf16[16,56,1024]{2,1,0:T(8,128)(2,1)S(1)} %bitcast.186), channel_id=1, replica_groups=mesh['section'=2,'fsdp'=2,'expert'=8] {'fsdp','expert'}, dimensions={0} | all-to-all | bytes 3670016 | tf_op jit(solution)/shard_map/all_to_all | solution.py:78
  82.8 4.6 fusion.27
  87.4 4.6 fusion.30
  92.0 3.1 pad_maximum_fusion
  97.1 66.9 %reduce-scatter.3.cloned.1.call-done = f32[8,4,14,1536]{3,0,2,1:T(8,128)} async-done(((f32[16,4,14,1536]{3,0,2,1:T(8,128)}), f32[8,4,14,1536]{3,0,2,1:T(8,128)}) %reduce-scatter.3.cloned.1.call-update) | async-done | bytes 2752528 | tf_op jit(solution)/shard_map/reduce_scatter | solution.py:83
  164.0 3.2 fusion.102
  167.9 16.5 %collective-permute-done.6 = bf16[1,8,4,14,768]{4,1,3,2,0:T(8,128)(2,1)S(1)} collective-permute-done((bf16[1,8,4,14,768]{4,1,3,2,0:T(8,128)(2,1)}, bf16[1,8,4,14,768]{4,1,3,2,0:T(8,128)(2,1)S(1)}, u32[]{:S(2)}, u32[]{:S(2)}) %collective-permute-start.6) | collective-permute-done | bytes 688160 | tf_op jit(solution)/shard_map/ppermute | solution.py:22
  184.8 4.6 fusion.24
  191.6 5.7 %all-to-all-start.1 = ((bf16[16,56,1024]{2,1,0:T(8,128)(2,1)}), bf16[16,56,1024]{2,1,0:T(8,128)(2,1)S(1)}, u32[]{:S(2)}, u32[]{:S(2)}) async-start(bf16[16,56,1024]{2,1,0:T(8,128)(2,1)} %copy.75), calls=%async_computation.2 | async-start | bytes 3670016 | tf_op jit(solution)/shard_map/all_to_all | solution.py:95
  201.3 39.1 %all-to-all-done.1 = bf16[16,56,1024]{2,1,0:T(8,128)(2,1)S(1)} async-done(((bf16[16,56,1024]{2,1,0:T(8,128)(2,1)}), bf16[16,56,1024]{2,1,0:T(8,128)(2,1)S(1)}, u32[]{:S(2)}, u32[]{:S(2)}) %all-to-all-start.1) | async-done | bytes 1835040 | tf_op jit(solution)/shard_map/all_to_all | solution.py:95
  246.8 4.3 multiply_reduce_fusion.1
  256.9 48.5 %all_to_all.21 = bf16[16,56,1024]{2,1,0:T(8,128)(2,1)S(1)} all-to-all(bf16[16,56,1024]{2,1,0:T(8,128)(2,1)S(1)} %bitcast.188), channel_id=1, replica_groups=mesh['section'=2,'fsdp'=2,'expert'=8] {'fsdp','expert'}, dimensions={0} | all-to-all | bytes 3670016 | tf_op jit(solution)/shard_map/all_to_all | solution.py:78
  306.4 6.4 %fusion.36 = f32[16,4,14,768]{3,0,2,1:T(8,128)S(1)} fusion(bf16[16,4,14,1024]{3,0,2,1:T(8,128)(2,1)S(1)} %bitcast.192, bf16[4,1024,768]{2,1,0:T(8,128)(2,1)} %collective-permute-done.4, pred[]{:T(512)S(6)} %eq.129, bf16[1,4,1024,768]{3,2,1,0:T(8,128)(2,1)} %param.12), kind=kOutput, calls=%fused_computation.38 | convolution fusion | flops 1412431872 | bytes 17170432 | tf_op jit(solution)/shard_map/sjcd,jdh->sjch/dot_general | solution.py:80
  312.8 6.4 %fusion.39 = f32[16,4,14,768]{3,0,2,1:T(8,128)S(1)} fusion(bf16[16,4,14,1024]{3,0,2,1:T(8,128)(2,1)S(1)} %bitcast.193, bf16[4,1024,768]{2,1,0:T(8,128)(2,1)} %collective-permute-done.5, pred[]{:T(512)S(6)} %eq.129, bf16[1,4,1024,768]{3,2,1,0:T(8,128)(2,1)} %param.13), kind=kOutput, calls=%fused_computation.39 | convolution fusion | flops 1412431872 | bytes 17170432 | tf_op jit(solution)/shard_map/sjcd,jdh->sjch/dot_general | solution.py:81
  319.2 3.1 pad_maximum_fusion.1
  322.4 66.3 %reduce-scatter.5.cloned.1.call-done = f32[8,4,14,1536]{3,0,2,1:T(8,128)} async-done(((f32[16,4,14,1536]{3,0,2,1:T(8,128)}), f32[8,4,14,1536]{3,0,2,1:T(8,128)}) %reduce-scatter.5.cloned.1.call-update) | async-done | bytes 2752528 | tf_op jit(solution)/shard_map/reduce_scatter | solution.py:83
  391.9 16.2 %collective-permute-done.7 = bf16[1,8,4,14,768]{4,1,3,2,0:T(8,128)(2,1)S(1)} collective-permute-done((bf16[1,8,4,14,768]{4,1,3,2,0:T(8,128)(2,1)S(1)}, bf16[1,8,4,14,768]{4,1,3,2,0:T(8,128)(2,1)S(1)}, u32[]{:S(2)}, u32[]{:S(2)}) %collective-permute-start.7) | collective-permute-done | bytes 688160 | tf_op jit(solution)/shard_map/ppermute | solution.py:22
  408.5 6.4 %fusion.33 = bf16[4,1024,16,14]{1,2,3,0:T(8,128)(2,1)S(1)} fusion(bf16[4,768,1024]{2,1,0:T(8,128)(2,1)} %collective-permute-done.3, pred[]{:T(512)S(6)} %eq.129, bf16[2,1,8,4,14,768]{5,2,4,3,1,0:T(8,128)(2,1)S(1)} %reverse_select_fusion, bf16[1,4,768,1024]{3,2,1,0:T(8,128)(2,1)} %param.14), kind=kOutput, calls=%fused_computation.37 | convolution fusion | flops 1413349376 | bytes 15794177 | tf_op jit(solution)/shard_map/sjch,jhd->sjcd/dot_general | solution.py:92
  417.2 6.0 %all-to-all-start.3 = ((bf16[16,56,1024]{2,1,0:T(8,128)(2,1)}), bf16[16,56,1024]{2,1,0:T(8,128)(2,1)S(1)}, u32[]{:S(2)}, u32[]{:S(2)}) async-start(bf16[16,56,1024]{2,1,0:T(8,128)(2,1)} %copy.87), calls=%async_computation.5 | async-start | bytes 3670016 | tf_op jit(solution)/shard_map/all_to_all | solution.py:95
  424.0 39.0 %all-to-all-done.3 = bf16[16,56,1024]{2,1,0:T(8,128)(2,1)S(1)} async-done(((bf16[16,56,1024]{2,1,0:T(8,128)(2,1)}), bf16[16,56,1024]{2,1,0:T(8,128)(2,1)S(1)}, u32[]{:S(2)}, u32[]{:S(2)}) %all-to-all-start.3) | async-done | bytes 1835040 | tf_op jit(solution)/shard_map/all_to_all | solution.py:95
  469.5 4.3 multiply_reduce_fusion
  475.9 39.4 %psum.7 = f32[2]{0:T(128)S(1)} all-reduce(f32[2]{0:T(128)S(1)} %pad_maximum_fusion.4), channel_id=1, replica_groups=mesh['section'=2,'fsdp'=2,'expert'=8] {'section','fsdp','expert'}, use_global_device_ids=true, to_apply=%region_20.22 | all-reduce | flops 2 | bytes 16 | tf_op jit(solution)/shard_map/psum | solution.py:136
  (119 shorter events, 50.7 us)
Async XLA Ops:
  7.2 156.8 %reduce-scatter.3.cloned.1.call-start = ((), (), s32[]{:S(2)}) async-start(), calls=%async_computation.6 | async-start | bytes 8257536 | tf_op jit(solution)/shard_map/reduce_scatter | solution.py:83
  7.2 75.6 %collective-permute-start.4 = (bf16[4,1024,768]{2,1,0:T(8,128)(2,1)}, bf16[4,1024,768]{2,1,0:T(8,128)(2,1)}, u32[]{:S(2)}, u32[]{:S(2)}) collective-permute-start(bf16[4,1024,768]{2,1,0:T(8,128)(2,1)} %bitcast.203), channel_id=1, source_target_pairs={{0,16},{16,0},{1,17},{17,1},{2,18},{18,2},{3,19},{19,3},{4,20},{20... | collective-permute-start | bytes 18874376 | tf_op jit(solution)/shard_map/ppermute | solution.py:31
  8.5 9.4 %collective-permute-start = (s32[128,6]{0,1:T(8,128)S(1)}, s32[128,6]{0,1:T(8,128)S(1)}, u32[]{:S(2)}, u32[]{:S(2)}) collective-permute-start(s32[128,6]{0,1:T(8,128)S(1)} %bitcast.202), channel_id=1, source_target_pairs={{0,16},{16,0},{1,17},{17,1},{2,18},{18,2},{3,19},{19,3},{4,20},{20... | collective-permute-start | bytes 9224 | tf_op jit(solution)/shard_map/ppermute | solution.py:31
  8.5 12.2 %collective-permute-start.1 = (f32[2048]{0:T(1024)}, f32[2048]{0:T(1024)S(1)}, u32[]{:S(2)}, u32[]{:S(2)}) collective-permute-start(f32[2048]{0:T(1024)} %bitcast.200), channel_id=1, source_target_pairs={{0,16},{16,0},{1,17},{17,1},{2,18},{18,2},{3,19},{19,3},{4,20},{20... | collective-permute-start | bytes 24584 | tf_op jit(solution)/shard_map/ppermute | solution.py:31
  9.0 78.4 %collective-permute-start.5 = (bf16[4,1024,768]{2,1,0:T(8,128)(2,1)}, bf16[4,1024,768]{2,1,0:T(8,128)(2,1)}, u32[]{:S(2)}, u32[]{:S(2)}) collective-permute-start(bf16[4,1024,768]{2,1,0:T(8,128)(2,1)} %bitcast.204), channel_id=1, source_target_pairs={{0,16},{16,0},{1,17},{17,1},{2,18},{18,2},{3,19},{19,3},{4,20},{20... | collective-permute-start | bytes 18874376 | tf_op jit(solution)/shard_map/ppermute | solution.py:31
  95.1 89.7 %collective-permute-start.3 = (bf16[4,768,1024]{2,1,0:T(8,128)(2,1)}, bf16[4,768,1024]{2,1,0:T(8,128)(2,1)}, u32[]{:S(2)}, u32[]{:S(2)}) collective-permute-start(bf16[4,768,1024]{2,1,0:T(8,128)(2,1)} %bitcast.205), channel_id=1, source_target_pairs={{0,16},{16,0},{1,17},{17,1},{2,18},{18,2},{3,19},{19,3},{4,20},{20... | collective-permute-start | bytes 18874376 | tf_op jit(solution)/shard_map/ppermute | solution.py:31
  164.0 3.5 copy-start
  167.2 17.2 %collective-permute-start.6 = (bf16[1,8,4,14,768]{4,1,3,2,0:T(8,128)(2,1)}, bf16[1,8,4,14,768]{4,1,3,2,0:T(8,128)(2,1)S(1)}, u32[]{:S(2)}, u32[]{:S(2)}) collective-permute-start(bf16[1,8,4,14,768]{4,1,3,2,0:T(8,128)(2,1)} %fusion.102), channel_id=1, source_target_pairs={{0,8},{8,0},{1,9},{9,1},{2,10},{10,2},{3,11},{11,3},{4,12},{12,4},... | collective-permute-start | bytes 2064392 | tf_op jit(solution)/shard_map/ppermute | solution.py:22
  191.6 6.3 %copy-start.6 = (bf16[1,2048,32]{1,2,0:T(8,128)(2,1)S(1)}, bf16[1,2048,32]{1,2,0:T(8,128)(2,1)}, u32[]{:S(2)}) copy-start(bf16[1,2048,32]{1,2,0:T(8,128)(2,1)} %param.11) | copy-start | bytes 393220
  191.6 9.2 %copy-start.4 = (bf16[128,2048]{1,0:T(8,128)(2,1)S(1)}, bf16[128,2048]{1,0:T(8,128)(2,1)}, u32[]{:S(2)}) copy-start(bf16[128,2048]{1,0:T(8,128)(2,1)} %param.9) | copy-start | bytes 1572868
  191.6 48.7 %all-to-all-start.1 = ((bf16[16,56,1024]{2,1,0:T(8,128)(2,1)}), bf16[16,56,1024]{2,1,0:T(8,128)(2,1)S(1)}, u32[]{:S(2)}, u32[]{:S(2)}) async-start(bf16[16,56,1024]{2,1,0:T(8,128)(2,1)} %copy.75), calls=%async_computation.2 | async-start | bytes 3670016 | tf_op jit(solution)/shard_map/all_to_all | solution.py:95
  197.4 191.3 %reduce-scatter.5.cloned.1.call-start = ((), (), s32[]{:S(2)}) async-start(), calls=%async_computation.7 | async-start | bytes 8257536 | tf_op jit(solution)/shard_map/reduce_scatter | solution.py:83
  198.0 2.9 collective-permute-start.2
  200.8 41.4 %copy-start.8 = (bf16[2048,32]{0,1:T(8,128)(2,1)}, bf16[2048,32]{0,1:T(8,128)(2,1)S(1)}, u32[]{:S(2)}) copy-start(bf16[2048,32]{0,1:T(8,128)(2,1)S(1)} %collective-permute-done.2) | copy-start | bytes 393220
  246.8 4.3 copy-start.5
  251.9 171.6 %copy-start.2 = (bf16[64,2048]{1,0:T(8,128)(2,1)}, bf16[64,2048]{1,0:T(8,128)(2,1)S(1)}, u32[]{:S(2)}) copy-start(bf16[64,2048]{1,0:T(8,128)(2,1)S(1)} %get-tuple-element.13) | copy-start | bytes 786436
  388.7 2.7 copy-start.1
  391.0 17.1 %collective-permute-start.7 = (bf16[1,8,4,14,768]{4,1,3,2,0:T(8,128)(2,1)S(1)}, bf16[1,8,4,14,768]{4,1,3,2,0:T(8,128)(2,1)S(1)}, u32[]{:S(2)}, u32[]{:S(2)}) collective-permute-start(bf16[1,8,4,14,768]{4,1,3,2,0:T(8,128)(2,1)S(1)} %fusion.100), channel_id=1, source_target_pairs={{0,8},{8,0},{1,9},{9,1},{2,10},{10,2},{3,11},{11,3},{4,12},{12,4},... | collective-permute-start | bytes 2064392 | tf_op jit(solution)/shard_map/ppermute | solution.py:22
  417.1 6.4 %copy-start.7 = (bf16[1,2048,32]{1,2,0:T(8,128)(2,1)S(1)}, bf16[1,2048,32]{1,2,0:T(8,128)(2,1)}, u32[]{:S(2)}) copy-start(bf16[1,2048,32]{1,2,0:T(8,128)(2,1)} %param.11) | copy-start | bytes 393220
  417.2 6.4 %copy-start.9 = (bf16[2048,32]{0,1:T(8,128)(2,1)S(1)}, bf16[2048,32]{0,1:T(8,128)(2,1)}, u32[]{:S(2)}) copy-start(bf16[2048,32]{0,1:T(8,128)(2,1)} %copy-done.8) | copy-start | bytes 393220
  417.2 45.9 %all-to-all-start.3 = ((bf16[16,56,1024]{2,1,0:T(8,128)(2,1)}), bf16[16,56,1024]{2,1,0:T(8,128)(2,1)S(1)}, u32[]{:S(2)}, u32[]{:S(2)}) async-start(bf16[16,56,1024]{2,1,0:T(8,128)(2,1)} %copy.87), calls=%async_computation.5 | async-start | bytes 3670016 | tf_op jit(solution)/shard_map/all_to_all | solution.py:95
  469.5 4.3 copy-start.3
  515.4 1.4 collective-permute-start.8
Sparse Core Ops, SparseCore 0:
  95.2 68.7 reduce-scatter.2
  322.5 66.1 reduce-scatter.4
